TPU v7x, 128 devices: a whole 4x4x4 slice. The times are simulated.
128 devices in a mesh: row: 16 (over z_lo, x, core), col: 8 (over y, z_hi).
Axes of the slice: x: 4, y: 4, z: 4 (z_hi: 2, z_lo: 2; z = z_hi * 2 + z_lo), core: 2. Of those that a mesh axis runs over, the one named last changes fastest.
Arguments:
- shared_rows: float32 [2048, 16384], P('row', 'col'), may hold values from -0.125 to 0.125
- event_counts: int32 [16], replicated, may hold values from 32 to 128, as said below
- ridge: float32 [16384], P('col'), may hold values from 0.5 to 2
- items: float32 [1024, 16384], P('row', 'col'), may hold values from -6 to 6
- cand_ids: int32 [512], replicated, may hold values from 0 to 1023
- theta: float32 [16384], P('col'), may hold values from -0.046875 to 0.046875
Outputs:
- gram_tile: float32 [16384, 16384], P('row', 'col')
- scores: float32 [512], replicated
Inputs may be any that keep to these rules, and one draw needn't show every extreme that they name: event_counts[s] counts the live slots at the start of row shard s's 128 slots; some shard is full.
All inputs are finite; a program needn't handle non-finite values.
Results may differ from a plain program's by a relative error of at most 0.000068.
Values sent between devices are 32-bit elements; how exact they have to be, the bound alone decides.
No kernel may reach another device: no remote copies, remote signals or barrier semaphores. Data moves between devices by JAX's collectives and lax.ppermute only.
A program may use at most 128 MiB of HBM per device.

v0:
```python
import jax
import jax.numpy as jnp
from jax import lax
from jax.sharding import PartitionSpec as P

F = 16384
high = lax.Precision.HIGHEST


def spread(value, axis, source):
    kept = jnp.where(lax.axis_index(axis) == source, value, 0).astype(value.dtype)
    return lax.psum(kept, axis)


def body(shared_rows, event_counts, ridge, items, cand_ids, theta):
    ratio = lax.axis_size("row") // lax.axis_size("col")
    row_pos = lax.axis_index("row")
    col_pos = lax.axis_index("col")
    width_col = shared_rows.shape[1]
    width_row = width_col // ratio
    ev_slots = shared_rows.shape[0]
    slot = lax.iota(jnp.int32, ev_slots)
    masked = jnp.where((slot < event_counts[row_pos])[:, None], shared_rows, jnp.float32(0.0))
    offset = row_pos % ratio * width_row
    root = row_pos // ratio
    contract = (((0,), (0,)), ((), ()))
    col_all = lax.all_gather(masked, "row", axis=0, tiled=True)
    row_all = spread(lax.dynamic_slice_in_dim(col_all, offset, width_row, 1), "col", root)
    tile = lax.dot_general(
        row_all, col_all, contract, precision=high, preferred_element_type=jnp.float32
    )
    rows_global = row_pos * width_row + lax.broadcasted_iota(jnp.int32, (width_row, width_col), 0)
    cols_global = col_pos * width_col + lax.broadcasted_iota(jnp.int32, (width_row, width_col), 1)
    tile = tile + jnp.where(rows_global == cols_global, ridge[None, :], jnp.float32(0.0))
    items_dev = items.shape[0]
    onehot = (
        cand_ids[:, None] == row_pos * items_dev + lax.iota(jnp.int32, items_dev)[None, :]
    ).astype(jnp.float32)
    picked = jnp.dot(onehot, items, precision=high, preferred_element_type=jnp.float32)
    cand_col = lax.psum(picked, "row")
    across = (((1,), (1,)), ((), ()))
    cand_row = spread(lax.dynamic_slice_in_dim(cand_col, offset, width_row, 1), "col", root)
    image_part = lax.dot_general(
        cand_col, tile, across, precision=high, preferred_element_type=jnp.float32
    )
    image_row = lax.psum(image_part, "col")
    quad = jnp.where(col_pos == 0, jnp.sum(cand_row * image_row, axis=1), jnp.float32(0.0))
    linear = jnp.where(
        row_pos == 0,
        jnp.dot(cand_col, theta, precision=high, preferred_element_type=jnp.float32),
        jnp.float32(0.0),
    )
    quad_all, linear_all = lax.psum((quad, linear), ("row", "col"))
    return (tile, linear_all + jnp.sqrt(quad_all / F))


def solution(mesh):
    return jax.shard_map(
        body,
        mesh=mesh,
        in_specs=(P("row", "col"), P(), P("col"), P("row", "col"), P(), P("col")),
        out_specs=(P("row", "col"), P()),
        check_vma=False,
    )
```

profile of v0, /device:TPU:1, one launch (start us, length us, event | category | flops | bytes accessed | tf_op | source)
XLA Modules:
  0.0 940.3 jit_solution(5957106584917055528)
XLA Ops:
  7.2 0.0 copy-start
  7.2 0.0 all-gather.2.cloned.1.call-start
  7.2 1.3 dynamic_slice.9
  8.5 0.6 iota_compare_fusion
  9.2 2.3 broadcast_select_fusion
  11.5 0.0 all-gather.2.cloned.1.call-update
  11.5 0.0 all-reduce.8.cloned.1.call-start
  11.6 0.0 copy-done
  11.6 4.5 fusion
  16.1 0.0 all-reduce.8.cloned.1.call-update
  16.1 0.0 all-reduce.6.cloned.1.call-start
  16.2 90.8 %all-gather.2.cloned.1.call-done = f32[2048,2048]{1,0:T(8,128)} async-done(((f32[128,2048]{1,0:T(8,128)}), f32[2048,2048]{1,0:T(8,128)}) %all-gather.2.cloned.1.call-update) | async-done | bytes 16777232 | tf_op jit(solution)/shard_map/all_gather | solution.py:27
  107.0 8.7 dynamic-slice_select_fusion
  115.7 0.0 copy-start.3
  115.7 0.0 all-reduce.6.cloned.1.call-update
  115.7 0.0 all-reduce.10.cloned.1.call-start
  115.8 122.9 %all-reduce.8.cloned.1.call-done = f32[512,2048]{1,0:T(8,128)} async-done(((f32[512,2048]{1,0:T(8,128)}), f32[512,2048]{1,0:T(8,128)}) %all-reduce.8.cloned.1.call-update) | async-done | bytes 4194320 | tf_op jit(solution)/shard_map/psum | solution.py:40
  238.7 3.2 dynamic-slice_select_fusion.1
  241.9 343.4 %all-reduce.6.cloned.1.call-done = f32[2048,1024]{1,0:T(8,128)} async-done(((f32[2048,1024]{1,0:T(8,128)}), f32[2048,1024]{1,0:T(8,128)}) %all-reduce.6.cloned.1.call-update) | async-done | bytes 8388624 | tf_op jit(solution)/shard_map/psum | solution.py:12
  585.3 0.0 copy-done.3
  585.3 67.7 %select_add_fusion = f32[1024,2048]{1,0:T(8,128)S(1)} fusion(f32[2048]{0:T(1024)S(1)} %copy-done.3, s32[2048]{0:T(1024)S(1)} %iota_add_fusion, s32[1024]{0:T(1024)S(1)} %iota_add_fusion.1, f32[2048,1024]{1,0:T(8,128)} %all-reduce.6.cloned.1.call-done, f32[2048,2048]{1,0:T(8,128)} %all-gather.2.cloned.1.call-done), kind=kOutput, calls=%fused_computation | convolution fusion | flops 51545899008 | bytes 33574912 | tf_op jit(solution)/shard_map/dot_general | solution.py:29
  653.1 0.0 copy-start.4
  653.1 3.4 copy-done.4
  656.5 0.0 copy-done.1
  656.5 15.2 %fusion.5 = f32[512,1024]{1,0:T(8,128)} fusion(f32[512,2048]{1,0:T(8,128)S(1)} %copy-done.1, f32[1024,2048]{1,0:T(8,128)S(1)} %select_add_fusion), kind=kOutput, calls=%fused_computation.17 | convolution fusion | flops 12884901888 | bytes 14680064 | tf_op jit(solution)/shard_map/dot_general | solution.py:43
  671.7 0.0 all-reduce.10.cloned.1.call-update
  671.7 0.0 copy-done.2
  671.7 5.8 fusion.4
  677.5 185.2 %all-reduce.10.cloned.1.call-done = (f32[512,1024]{1,0:T(8,128)}, f32[512,1024]{1,0:T(8,128)}) async-done(((f32[512,1024]{1,0:T(8,128)}, f32[512,1024]{1,0:T(8,128)}), (f32[512,1024]{1,0:T(8,128)}, f32[512,1024]{1,0:T(8,128)})) %all-reduce.10.cloned.1.call-update) | async-done | bytes 4194320 | tf_op jit(solution)/shard_map/psum | solution.py:12
  862.7 2.5 multiply_reduce_fusion
  865.2 67.8 %all-reduce = (f32[512]{0:T(512)S(1)}, f32[512]{0:T(512)S(1)}) all-reduce(f32[512]{0:T(512)S(1)} %broadcast_select_fusion.2, f32[512]{0:T(512)S(1)} %broadcast_select_fusion.1), channel_id=1, replica_groups=mesh['row'=16,'col'=8] {'row','col'}, use_global_device_ids=true, to_apply=%region_2.3 | all-reduce | flops 1024 | bytes 8192 | tf_op jit(solution)/shard_map/psum | solution.py:53
  933.0 0.6 sqrt_add_fusion
  (7 shorter events, 0.0 us)
Async XLA Ops:
  7.2 4.4 copy-start
  7.2 99.8 %all-gather.2.cloned.1.call-start = ((), (), s32[]{:S(2)}) async-start(), calls=%async_computation | async-start | bytes 17825792 | tf_op jit(solution)/shard_map/all_gather | solution.py:27
  11.5 227.2 %all-reduce.8.cloned.1.call-start = ((), (), s32[]{:S(2)}) async-start(), calls=%async_computation.2 | async-start | bytes 8388608 | tf_op jit(solution)/shard_map/psum | solution.py:40
  16.1 569.2 %all-reduce.6.cloned.1.call-start = ((), (), s32[]{:S(2)}) async-start(), calls=%async_computation.1 | async-start | bytes 16777216 | tf_op jit(solution)/shard_map/psum | solution.py:12
  115.7 469.7 %copy-start.3 = (f32[2048]{0:T(1024)S(1)}, f32[2048]{0:T(1024)}, u32[]{:S(2)}) copy-start(f32[2048]{0:T(1024)} %param.8) | copy-start | bytes 24580
  115.7 747.0 %all-reduce.10.cloned.1.call-start = ((), (), s32[]{:S(2)}) async-start(), calls=%async_computation.3 | async-start | bytes 8388608 | tf_op jit(solution)/shard_map/psum | solution.py:12
  585.3 71.1 %copy-start.1 = (f32[512,2048]{1,0:T(8,128)S(1)}, f32[512,2048]{1,0:T(8,128)}, u32[]{:S(2)}) copy-start(f32[512,2048]{1,0:T(8,128)} %all-reduce.8.cloned.1.call-done) | copy-start | bytes 12582916
  653.1 3.4 copy-start.4
  656.5 15.3 %copy-start.2 = (f32[2048]{0:T(1024)S(1)}, f32[2048]{0:T(1024)}, u32[]{:S(2)}) copy-start(f32[2048]{0:T(1024)} %param.11) | copy-start | bytes 24580
Sparse Core Ops, SparseCore 0:
  11.7 95.2 all-gather.1
  109.5 129.1 all-reduce.7
  241.8 343.4 all-reduce.5
  671.8 190.8 all-reduce.9
where the time goes:
time: 944 us; the launch traced here: 940 us
  waiting for transfers between devices  742 us (79%)
  matrix products  93.2 us (10%)
  blocking collectives  67.8 us (7%)
  other arithmetic  18 us (2%)
  between operations  14.1 us (1%)
    psum x2, waiting for transfers between devices, spread(): return lax.psum(kept, axis)  529 us
    psum x1, waiting for transfers between devices, body(): cand_col = lax.psum(picked, 'row')  123 us
    all_gather x1, waiting for transfers between devices, body(): col_all = lax.all_gather(masked, 'row', axis=0, tiled=True)  90.8 us
    psum x1, blocking collectives, body(): quad_all, linear_all = lax.psum((quad, linear), ('row', 'col'))  67.8 us
    dot_general x1, matrix products, body(): lax.dot_general(row_all, col_all, contract, precision=high, preferred_ele...  67.7 us
  transfers between devices with their start and end apart: 4, of which 4 were waited for; matrix products, arithmetic and copies ran while one was open for 2% of the time, Pallas kernels for 0%

commit v1 on v0

--- a/solution.py
+++ b/solution.py
@@ -50,7 +50,7 @@
         jnp.dot(cand_col, theta, precision=high, preferred_element_type=jnp.float32),
         jnp.float32(0.0),
     )
-    quad_all, linear_all = lax.psum((quad, linear), ("row", "col"))
+    quad_all, linear_all = lax.psum(lax.psum((quad, linear), "col"), "row")
     return (tile, linear_all + jnp.sqrt(quad_all / F))
 
 

time: 944 us -> 914 us (0.968)
  blocking collectives: 67.8 us -> 50.5 us
    psum x1 -> x2, blocking collectives: 67.8 us -> 50.5 us  [body(): quad_all, linear_all = lax.psum(lax.psum((quad, linear), 'col'), 'row')]
where the time goes in v1:
time: 914 us
  waiting for transfers between devices  742 us (81%)
  matrix products  84.4 us (9%)
  blocking collectives  50.5 us (6%)
  other arithmetic  18 us (2%)
  between operations  13.9 us (2%)
    psum x2, waiting for transfers between devices, spread(): return lax.psum(kept, axis)  529 us
    psum x1, waiting for transfers between devices, body(): cand_col = lax.psum(picked, 'row')  123 us
    all_gather x1, waiting for transfers between devices, body(): col_all = lax.all_gather(masked, 'row', axis=0, tiled=True)  90.8 us
    dot_general x1, matrix products, body(): lax.dot_general(row_all, col_all, contract, precision=high, preferred_ele...  58.9 us
    psum x2, blocking collectives, body(): quad_all, linear_all = lax.psum(lax.psum((quad, linear), 'col'), 'row')  50.5 us
  transfers between devices with their start and end apart: 4, of which 4 were waited for; matrix products, arithmetic and copies ran while one was open for 2% of the time, Pallas kernels for 0%

profile of v1, /device:TPU:1, one launch (start us, length us, event | category | flops | bytes accessed | tf_op | source)
XLA Modules:
  0.0 913.9 jit_solution(10166430245544360324)
XLA Ops:
  7.2 0.0 copy-start
  7.2 0.0 all-gather.2.cloned.1.call-start
  7.2 1.3 dynamic_slice.9
  8.5 0.6 iota_compare_fusion
  9.2 2.3 broadcast_select_fusion
  11.5 0.0 all-gather.2.cloned.1.call-update
  11.5 0.0 all-reduce.9.cloned.1.call-start
  11.6 0.0 copy-done
  11.6 4.5 fusion
  16.1 0.0 all-reduce.9.cloned.1.call-update
  16.1 0.0 all-reduce.7.cloned.1.call-start
  16.2 90.8 %all-gather.2.cloned.1.call-done = f32[2048,2048]{1,0:T(8,128)} async-done(((f32[128,2048]{1,0:T(8,128)}), f32[2048,2048]{1,0:T(8,128)}) %all-gather.2.cloned.1.call-update) | async-done | bytes 16777232 | tf_op jit(solution)/shard_map/all_gather | solution.py:27
  107.0 8.7 dynamic-slice_select_fusion
  115.7 0.0 all-reduce.7.cloned.1.call-update
  115.7 0.0 all-reduce.11.cloned.1.call-start
  115.8 122.9 %all-reduce.9.cloned.1.call-done = f32[512,2048]{1,0:T(8,128)} async-done(((f32[512,2048]{1,0:T(8,128)}), f32[512,2048]{1,0:T(8,128)}) %all-reduce.9.cloned.1.call-update) | async-done | bytes 4194320 | tf_op jit(solution)/shard_map/psum | solution.py:40
  238.7 3.2 dynamic-slice_select_fusion.1
  241.9 343.4 %all-reduce.7.cloned.1.call-done = f32[2048,1024]{1,0:T(8,128)} async-done(((f32[2048,1024]{1,0:T(8,128)}), f32[2048,1024]{1,0:T(8,128)}) %all-reduce.7.cloned.1.call-update) | async-done | bytes 8388624 | tf_op jit(solution)/shard_map/psum | solution.py:12
  585.3 0.0 copy-done.3
  585.3 58.9 %select_add_fusion = f32[1024,2048]{1,0:T(8,128)S(1)} fusion(f32[2048]{0:T(1024)S(1)} %copy-done.3, s32[2048]{0:T(1024)S(1)} %iota_add_fusion, s32[1024]{0:T(1024)S(1)} %iota_add_fusion.1, f32[2048,1024]{1,0:T(8,128)} %all-reduce.7.cloned.1.call-done, f32[2048,2048]{1,0:T(8,128)} %all-gather.2.cloned.1.call-done), kind=kOutput, calls=%fused_computation | convolution fusion | flops 51545899008 | bytes 33574912 | tf_op jit(solution)/shard_map/dot_general | solution.py:29
  644.2 0.0 copy-start.4
  644.2 3.4 copy-done.4
  647.6 0.0 copy-done.1
  647.6 15.3 %fusion.5 = f32[512,1024]{1,0:T(8,128)} fusion(f32[512,2048]{1,0:T(8,128)S(1)} %copy-done.1, f32[1024,2048]{1,0:T(8,128)S(1)} %select_add_fusion), kind=kOutput, calls=%fused_computation.17 | convolution fusion | flops 12884901888 | bytes 14680064 | tf_op jit(solution)/shard_map/dot_general | solution.py:43
  662.9 0.0 all-reduce.11.cloned.1.call-update
  662.9 0.0 copy-done.2
  662.9 5.8 fusion.4
  668.7 185.1 %all-reduce.11.cloned.1.call-done = (f32[512,1024]{1,0:T(8,128)}, f32[512,1024]{1,0:T(8,128)}) async-done(((f32[512,1024]{1,0:T(8,128)}, f32[512,1024]{1,0:T(8,128)}), (f32[512,1024]{1,0:T(8,128)}, f32[512,1024]{1,0:T(8,128)})) %all-reduce.11.cloned.1.call-update) | async-done | bytes 4194320 | tf_op jit(solution)/shard_map/psum | solution.py:12
  853.8 2.5 multiply_reduce_fusion
  856.3 18.9 %all-reduce.1 = (f32[512]{0:T(512)S(1)}, f32[512]{0:T(512)S(1)}) all-reduce(f32[512]{0:T(512)S(1)} %broadcast_select_fusion.2, f32[512]{0:T(512)S(1)} %broadcast_select_fusion.1), channel_id=1, replica_groups=mesh['row'=16,'col'=8] {'col'}, use_global_device_ids=true, to_apply=%region_2.3 | all-reduce | flops 1024 | bytes 8192 | tf_op jit(solution)/shard_map/psum | solution.py:53
  875.2 31.6 %all-reduce = (f32[512]{0:T(512)S(1)}, f32[512]{0:T(512)S(1)}) all-reduce(f32[512]{0:T(512)S(1)} %get-tuple-element.4, f32[512]{0:T(512)S(1)} %get-tuple-element.5), channel_id=1, replica_groups=mesh['row'=16,'col'=8] {'row'}, use_global_device_ids=true, to_apply=%region_3.4 | all-reduce | flops 1024 | bytes 8192 | tf_op jit(solution)/shard_map/psum | solution.py:53
  906.8 0.6 sqrt_add_fusion
  (8 shorter events, 0.0 us)
Async XLA Ops:
  7.2 4.4 copy-start
  7.2 99.8 %all-gather.2.cloned.1.call-start = ((), (), s32[]{:S(2)}) async-start(), calls=%async_computation | async-start | bytes 17825792 | tf_op jit(solution)/shard_map/all_gather | solution.py:27
  11.5 227.2 %all-reduce.9.cloned.1.call-start = ((), (), s32[]{:S(2)}) async-start(), calls=%async_computation.2 | async-start | bytes 8388608 | tf_op jit(solution)/shard_map/psum | solution.py:40
  16.1 569.2 %all-reduce.7.cloned.1.call-start = ((), (), s32[]{:S(2)}) async-start(), calls=%async_computation.1 | async-start | bytes 16777216 | tf_op jit(solution)/shard_map/psum | solution.py:12
  115.7 469.7 %copy-start.3 = (f32[2048]{0:T(1024)S(1)}, f32[2048]{0:T(1024)}, u32[]{:S(2)}) copy-start(f32[2048]{0:T(1024)} %param.8) | copy-start | bytes 24580
  115.7 738.2 %all-reduce.11.cloned.1.call-start = ((), (), s32[]{:S(2)}) async-start(), calls=%async_computation.3 | async-start | bytes 8388608 | tf_op jit(solution)/shard_map/psum | solution.py:12
  585.3 62.3 %copy-start.1 = (f32[512,2048]{1,0:T(8,128)S(1)}, f32[512,2048]{1,0:T(8,128)}, u32[]{:S(2)}) copy-start(f32[512,2048]{1,0:T(8,128)} %all-reduce.9.cloned.1.call-done) | copy-start | bytes 12582916
  644.2 3.4 copy-start.4
  647.6 15.3 %copy-start.2 = (f32[2048]{0:T(1024)S(1)}, f32[2048]{0:T(1024)}, u32[]{:S(2)}) copy-start(f32[2048]{0:T(1024)} %param.11) | copy-start | bytes 24580
Sparse Core Ops, SparseCore 0:
  11.7 95.2 all-gather.1
  109.5 129.1 all-reduce.8
  241.8 343.4 all-reduce.6
  663.0 190.7 all-reduce.10
